TPU v7x, 256 devices: a whole 4x4x8 slice. The times are simulated.
256 devices in a mesh: sector: 64 (over z, y, core), dof: 4 (over x).
Axes of the slice: x: 4, y: 4, z: 8, core: 2. Of those that a mesh axis runs over, the one named last changes fastest.
Arguments:
- load_history: bfloat16 [64, 64, 6144], P('sector', None, 'dof'), may hold values from -6 to 6
- sector_basis: bfloat16 [6144, 1536], P('dof'), may hold values from -0.078125 to 0.078125
- harmonic_modes: bfloat16 [64, 1536, 256], P('sector'), may hold values from -0.15625 to 0.15625
- stress_basis: bfloat16 [1536, 6144], P(None, 'dof'), may hold values from -0.375 to 0.375
- mode_decay: float32 [64, 256], P('sector'), may hold values from 0.01 to 0.3
- mode_phase: float32 [64, 256], P('sector'), may hold values from 0.05 to 1.5
- mode_count: int32 [64], P('sector'), may hold values from 64 to 256, as said below
- slot_harmonic: int32 [64], replicated, may hold values from 0 to 63, each once
Outputs:
- stress_field: bfloat16 [64, 64, 6144], P('sector', None, 'dof')
Inputs may be any that keep to these rules, and one draw needn't show every extreme that they name: Slot modes from mode_count on are left out; some slot has 256 live modes and some 256 // 4. `slot_harmonic`: every harmonic component is held by exactly one slot.
All inputs are finite; a program needn't handle non-finite values.
Results may differ from a plain program's by a relative error of at most 0.025.
Values may be sent and summed in bfloat16 or wider, within the bound.
No kernel may reach another device: no remote copies, remote signals or barrier semaphores. Data moves between devices by JAX's collectives and lax.ppermute only.
A program may use at most 64 MiB of HBM per device.

v0:
```python
import math
import jax
import jax.numpy as jnp
from jax import lax
from jax.sharding import PartitionSpec as P


def transform_table(slot_harmonic):
    count_all = slot_harmonic.shape[0]
    half_count = count_all // 2
    sine_rows = slot_harmonic > half_count
    harmonic_order = jnp.where(sine_rows, slot_harmonic - half_count, slot_harmonic)
    sector_index = jnp.arange(count_all, dtype=jnp.int32)
    residue = harmonic_order[:, None] * sector_index[None, :] % count_all
    phase_angle = residue.astype(jnp.float32) * jnp.float32(2.0 * math.pi / count_all)
    wave_table = jnp.where(sine_rows[:, None], jnp.sin(phase_angle), jnp.cos(phase_angle))
    single = (slot_harmonic == 0) | (slot_harmonic == half_count)
    weight = jnp.where(single, jnp.float32(1.0 / count_all), jnp.float32(2.0 / count_all))
    return jnp.sqrt(weight)[:, None] * wave_table


def filter_kernel(decay_rates, phase_steps, steps_count):
    time_index = jnp.arange(steps_count, dtype=jnp.int32)
    offset = time_index[:, None] - time_index[None, :]
    causal = offset >= 0
    lag_value = jnp.maximum(offset, 0).astype(jnp.float32)
    gain_factor = jnp.sqrt(1.0 - jnp.exp(-2.0 * decay_rates))
    shape_table = (
        gain_factor[..., None, None]
        * jnp.exp(-decay_rates[..., None, None] * lag_value)
        * jnp.cos(phase_steps[..., None, None] * lag_value)
    )
    return jnp.where(causal, shape_table, jnp.float32(0.0))


def local(
    load_history,
    sector_basis,
    harmonic_modes,
    stress_basis,
    mode_decay,
    mode_phase,
    mode_count,
    slot_harmonic,
):
    highest = lax.Precision.HIGHEST
    table = transform_table(slot_harmonic)
    steps_count = load_history.shape[1]
    modes_slot = harmonic_modes[0]
    partial_value = jnp.dot(load_history[0], sector_basis, preferred_element_type=jnp.float32)
    live = (jnp.arange(modes_slot.shape[1], dtype=jnp.int32) < mode_count[0]).astype(jnp.float32)
    kernel = filter_kernel(mode_decay[0], mode_phase[0], steps_count)
    reduced = lax.psum(partial_value.astype(jnp.bfloat16), "dof")
    mixed = jnp.einsum(
        "ks,stc->ktc",
        table,
        lax.all_to_all(reduced[None], "sector", split_axis=1, concat_axis=0, tiled=True).astype(
            jnp.float32
        ),
        precision=highest,
    )
    spectrum = lax.all_to_all(
        mixed.astype(jnp.bfloat16), "sector", split_axis=0, concat_axis=1, tiled=True
    )[0]
    modal = jnp.dot(spectrum, modes_slot, preferred_element_type=jnp.float32) * live[None, :]
    response = jnp.einsum("mtu,um->tm", kernel, modal, precision=highest)
    project_response = response.astype(jnp.bfloat16)
    product = lax.dot_general(
        project_response, modes_slot, (((1,), (1,)), ((), ())), preferred_element_type=jnp.float32
    )
    returned = product.astype(jnp.bfloat16)
    mixed = jnp.einsum(
        "ks,ktc->stc",
        table,
        lax.all_to_all(returned[None], "sector", split_axis=1, concat_axis=0, tiled=True).astype(
            jnp.float32
        ),
        precision=highest,
    )
    back = lax.all_to_all(
        mixed.astype(jnp.bfloat16), "sector", split_axis=0, concat_axis=1, tiled=True
    )[0]
    stress_field = jnp.dot(back, stress_basis, preferred_element_type=jnp.float32).astype(
        jnp.bfloat16
    )
    return stress_field[None]


def solution(mesh):
    return jax.shard_map(
        local,
        mesh=mesh,
        in_specs=(
            P("sector", None, "dof"),
            P("dof", None),
            P("sector", None, None),
            P(None, "dof"),
            P("sector", None),
            P("sector", None),
            P("sector"),
            P(),
        ),
        out_specs=P("sector", None, "dof"),
        check_vma=False,
    )
```

profile of v0, /device:TPU:1, one launch (start us, length us, event | category | flops | bytes accessed | tf_op | source)
XLA Modules:
  0.0 171.5 jit_solution(9315487925137367451)
XLA Ops:
  6.5 0.0 all-reduce.2.cloned.1.call-start
  6.5 4.1 %fusion.3 = bf16[1,64,1536]{2,1,0:T(8,128)(2,1)} fusion(bf16[1536,1536]{1,0:T(8,128)(2,1)} %param.9, bf16[1,64,1536]{2,1,0:T(8,128)(2,1)} %param.8), kind=kOutput, calls=%fused_computation.9 | convolution fusion | flops 302088192 | bytes 5111808 | tf_op jit(solution)/shard_map/dot_general | solution.py:50
  10.7 0.0 all-reduce.2.cloned.1.call-update
  10.7 48.4 %all-reduce.2.cloned.1.call-done = bf16[1,64,1536]{2,1,0:T(8,128)(2,1)} async-done(((bf16[1,64,1536]{2,1,0:T(8,128)(2,1)}), bf16[1,64,1536]{2,1,0:T(8,128)(2,1)}) %all-reduce.2.cloned.1.call-update) | async-done | bytes 196624 | tf_op jit(solution)/shard_map/psum | solution.py:53
  59.1 1.2 copy.52
  60.3 0.6 broadcast.55
  60.9 1.8 %reduce.2 = bf16[64,1536]{1,0:T(8,128)(2,1)S(1)} reduce(bf16[64,1,1536]{2,1,0:T(2,128)(2,1)S(1)} %bitcast.50, bf16[]{:T(256)} %broadcast.55), dimensions={1}, to_apply=%bitcast.48.reduce_sub_computation | reduce | bytes 393218
  62.8 0.7 reshape.75
  63.5 12.8 %all-to-all-start = ((bf16[64,2,768]{2,1,0:T(2,128)(2,1)}), bf16[64,2,768]{2,1,0:T(2,128)(2,1)S(1)}, u32[]{:S(2)}, u32[]{:S(2)}) async-start(bf16[64,2,768]{2,1,0:T(2,128)(2,1)} %reshape.75), calls=%async_computation | async-start | bytes 393216 | tf_op jit(solution)/shard_map/all_to_all | solution.py:57
  77.0 11.3 %all-to-all-done = bf16[64,2,768]{2,1,0:T(2,128)(2,1)S(1)} async-done(((bf16[64,2,768]{2,1,0:T(2,128)(2,1)}), bf16[64,2,768]{2,1,0:T(2,128)(2,1)S(1)}, u32[]{:S(2)}, u32[]{:S(2)}) %all-to-all-start) | async-done | bytes 196640 | tf_op jit(solution)/shard_map/all_to_all | solution.py:57
  88.3 0.1 reshape.76
  88.5 0.5 fusion
  89.0 0.8 reduce.3
  89.8 0.7 reshape.77
  90.5 4.5 %all-to-all-start.1 = ((bf16[64,2,768]{2,1,0:T(2,128)(2,1)}), bf16[64,2,768]{2,1,0:T(2,128)(2,1)S(1)}, u32[]{:S(2)}, u32[]{:S(2)}) async-start(bf16[64,2,768]{2,1,0:T(2,128)(2,1)} %reshape.77), calls=%async_computation.1 | async-start | bytes 393216 | tf_op jit(solution)/shard_map/all_to_all | solution.py:62
  95.0 12.1 %all-to-all-done.1 = bf16[64,2,768]{2,1,0:T(2,128)(2,1)S(1)} async-done(((bf16[64,2,768]{2,1,0:T(2,128)(2,1)}), bf16[64,2,768]{2,1,0:T(2,128)(2,1)S(1)}, u32[]{:S(2)}, u32[]{:S(2)}) %all-to-all-start.1) | async-done | bytes 196640 | tf_op jit(solution)/shard_map/all_to_all | solution.py:62
  107.1 0.1 reshape.78
  107.2 0.2 fusion.5
  107.5 16.2 %multiply_reduce_fusion = bf16[256,64]{0,1:T(8,128)(2,1)S(1)} fusion(f32[256,64]{0,1:T(8,128)S(1)} %fusion.5, f32[256]{0:T(256)S(1)} %bitcast.56, f32[64,64]{1,0:T(8,128)S(1)} %maximum_convert_fusion, f32[256]{0:T(256)S(1)} %bitcast.55, f32[256]{0:T(256)S(1)} %bitcast.54, pred[64,64]{1,0:T(8,128)(4,1)S(1)} %fusion.21), kind=kLoop, calls=%fused_computation | loop fusion | flops 7323648 | bytes 121856
  123.8 0.1 copy.27
  123.9 0.4 fusion.1
  124.2 0.3 copy.51
  124.6 1.8 %reduce.4 = bf16[64,1536]{1,0:T(8,128)(2,1)S(1)} reduce(bf16[64,1,1536]{2,1,0:T(2,128)(2,1)S(1)} %bitcast.51, bf16[]{:T(256)} %broadcast.55), dimensions={1}, to_apply=%bitcast.47.reduce_sub_computation | reduce | bytes 393218
  126.4 0.1 reshape.79
  126.5 16.2 %all_to_all.16 = bf16[64,2,768]{2,1,0:T(2,128)(2,1)S(1)} all-to-all(bf16[64,2,768]{2,1,0:T(2,128)(2,1)S(1)} %reshape.79), channel_id=1, replica_groups=mesh['sector'=64,'dof'=4] {'sector'}, dimensions={0} | all-to-all | bytes 393216 | tf_op jit(solution)/shard_map/all_to_all | solution.py:75
  142.7 0.1 reshape.80
  142.8 0.6 fusion.2
  143.4 0.8 reduce.5
  144.2 0.1 reshape.81
  144.3 16.3 %all_to_all.17 = bf16[64,2,768]{2,1,0:T(2,128)(2,1)S(1)} all-to-all(bf16[64,2,768]{2,1,0:T(2,128)(2,1)S(1)} %reshape.81), channel_id=1, replica_groups=mesh['sector'=64,'dof'=4] {'sector'}, dimensions={0} | all-to-all | bytes 393216 | tf_op jit(solution)/shard_map/all_to_all | solution.py:80
  160.6 0.1 reshape.82
  160.7 3.9 %fusion.4 = bf16[1,64,1536]{2,1,0:T(8,128)(2,1)} fusion(bf16[1536,1536]{1,0:T(8,128)(2,1)} %param.11, bf16[64,1,1536]{2,1,0:T(2,128)(2,1)S(1)} %reshape.82), kind=kOutput, calls=%fused_computation.10 | convolution fusion | flops 302088192 | bytes 5111808 | tf_op jit(solution)/shard_map/dot_general | solution.py:83
  (15 shorter events, 0.1 us)
Async XLA Ops:
  6.5 100.7 %copy-start = (bf16[1,1536,256]{2,1,0:T(8,128)(2,1)S(1)}, bf16[1,1536,256]{2,1,0:T(8,128)(2,1)}, u32[]{:S(2)}) copy-start(bf16[1,1536,256]{2,1,0:T(8,128)(2,1)} %param.10) | copy-start | bytes 2359300
  6.5 4.2 %copy-start.3 = (s32[64]{0:T(128)S(1)}, s32[64]{0:T(128)}, u32[]{:S(2)}) copy-start(s32[64]{0:T(128)} %param.15) | copy-start | bytes 772
  6.5 88.4 %copy-start.1 = (f32[1,256]{1,0:T(1,128)S(1)}, f32[1,256]{1,0:T(1,128)}, u32[]{:S(2)}) copy-start(f32[1,256]{1,0:T(1,128)} %param.12) | copy-start | bytes 3076
  6.5 52.5 %all-reduce.2.cloned.1.call-start = ((), (), s32[]{:S(2)}) async-start(), calls=%async_computation.4 | async-start | bytes 393216 | tf_op jit(solution)/shard_map/psum | solution.py:53
  10.7 96.8 %copy-start.2 = (f32[1,256]{1,0:T(1,128)S(1)}, f32[1,256]{1,0:T(1,128)}, u32[]{:S(2)}) copy-start(f32[1,256]{1,0:T(1,128)} %param.13) | copy-start | bytes 3076
  63.5 24.8 %all-to-all-start = ((bf16[64,2,768]{2,1,0:T(2,128)(2,1)}), bf16[64,2,768]{2,1,0:T(2,128)(2,1)S(1)}, u32[]{:S(2)}, u32[]{:S(2)}) async-start(bf16[64,2,768]{2,1,0:T(2,128)(2,1)} %reshape.75), calls=%async_computation | async-start | bytes 393216 | tf_op jit(solution)/shard_map/all_to_all | solution.py:57
  90.5 16.6 %all-to-all-start.1 = ((bf16[64,2,768]{2,1,0:T(2,128)(2,1)}), bf16[64,2,768]{2,1,0:T(2,128)(2,1)S(1)}, u32[]{:S(2)}, u32[]{:S(2)}) async-start(bf16[64,2,768]{2,1,0:T(2,128)(2,1)} %reshape.77), calls=%async_computation.1 | async-start | bytes 393216 | tf_op jit(solution)/shard_map/all_to_all | solution.py:62
Sparse Core Ops, SparseCore 0:
  10.8 48.2 all-reduce.1
where the time goes:
time: 172 us; the launch traced here: 171 us
  waiting for transfers between devices  71.8 us (42%)
  blocking collectives  32.5 us (19%)
  other arithmetic  21.5 us (12%)
  starting transfers between devices  17.3 us (10%)
  between operations  14.2 us (8%)
  matrix products  9.72 us (6%)
  local copies, waits for them, and re-layouts  4.4 us (3%)
    psum x1, waiting for transfers between devices, local(): reduced = lax.psum(partial_value.astype(jnp.bfloat16), 'dof')  48.4 us
    unnamed x3, other arithmetic  19.9 us
    all_to_all x1, blocking collectives, local(): lax.all_to_all(mixed.astype(jnp.bfloat16), 'sector', split_axis=0, concat...  16.3 us
    all_to_all x1, blocking collectives, local(): lax.all_to_all(returned[None], 'sector', split_axis=1, concat_axis=0, til...  16.2 us
    all_to_all x1, starting transfers between devices, local(): lax.all_to_all(reduced[None], 'sector', split_axis=1, concat_axis=0, tile...  12.8 us
    all_to_all x1, waiting for transfers between devices, local(): lax.all_to_all(mixed.astype(jnp.bfloat16), 'sector', split_axis=0, concat...  12.1 us
    all_to_all x1, waiting for transfers between devices, local(): lax.all_to_all(reduced[None], 'sector', split_axis=1, concat_axis=0, tile...  11.3 us
    all_to_all x1, starting transfers between devices, local(): lax.all_to_all(mixed.astype(jnp.bfloat16), 'sector', split_axis=0, concat...  4.47 us
  transfers between devices with their start and end apart: 3, of which 3 were waited for; matrix products, arithmetic and copies ran while one was open for 0% of the time, Pallas kernels for 0%

commit v1 on v0

--- a/solution.py
+++ b/solution.py
@@ -50,7 +50,7 @@
     partial_value = jnp.dot(load_history[0], sector_basis, preferred_element_type=jnp.float32)
     live = (jnp.arange(modes_slot.shape[1], dtype=jnp.int32) < mode_count[0]).astype(jnp.float32)
     kernel = filter_kernel(mode_decay[0], mode_phase[0], steps_count)
-    reduced = lax.psum(partial_value.astype(jnp.bfloat16), "dof")
+    reduced = jnp.sum(lax.all_gather(partial_value.astype(jnp.bfloat16), "dof"), axis=0)
     mixed = jnp.einsum(
         "ks,stc->ktc",
         table,

time: 172 us -> 123 us (0.72)
  waiting for transfers between devices: 71.8 us -> 23.5 us
  between operations: 14.2 us -> 0.87 us
  blocking collectives: 32.5 us -> 45.4 us
    psum x1 -> x0, waiting for transfers between devices: 48.4 us -> none  [local(): reduced = lax.psum(partial_value.astype(jnp.bfloat16), 'dof')]
    all_gather x0 -> x1, blocking collectives: none -> 12.9 us  [local(): lax.all_gather(partial_value.astype(jnp.bfloat16), 'dof')]
  transfers between devices with their start and end apart: 3 -> 2, of which waited for: 3 -> 2; matrix products, arithmetic and copies ran while one was open for 0% -> 0% of each run, Pallas kernels for 0% -> 0%
where the time goes in v1:
time: 123 us; the launch traced here: 122 us
  blocking collectives  45.4 us (37%)
  waiting for transfers between devices  23.5 us (19%)
  other arithmetic  21.6 us (18%)
  starting transfers between devices  18.3 us (15%)
  matrix products  9.05 us (7%)
  local copies, waits for them, and re-layouts  3.48 us (3%)
    unnamed x3, other arithmetic  19.9 us
    all_to_all x1, blocking collectives, local(): lax.all_to_all(mixed.astype(jnp.bfloat16), 'sector', split_axis=0, concat...  16.3 us
    all_to_all x1, blocking collectives, local(): lax.all_to_all(returned[None], 'sector', split_axis=1, concat_axis=0, til...  16.2 us
    all_to_all x1, starting transfers between devices, local(): lax.all_to_all(reduced[None], 'sector', split_axis=1, concat_axis=0, tile...  13.9 us
    all_gather x1, blocking collectives, local(): lax.all_gather(partial_value.astype(jnp.bfloat16), 'dof')  12.9 us
    all_to_all x1, waiting for transfers between devices, local(): lax.all_to_all(mixed.astype(jnp.bfloat16), 'sector', split_axis=0, concat...  12.2 us
    all_to_all x1, waiting for transfers between devices, local(): lax.all_to_all(reduced[None], 'sector', split_axis=1, concat_axis=0, tile...  11.3 us
    all_to_all x1, starting transfers between devices, local(): lax.all_to_all(mixed.astype(jnp.bfloat16), 'sector', split_axis=0, concat...  4.47 us
  transfers between devices with their start and end apart: 2, of which 2 were waited for; matrix products, arithmetic and copies ran while one was open for 0% of the time, Pallas kernels for 0%

profile of v1, /device:TPU:1, one launch (start us, length us, event | category | flops | bytes accessed | tf_op | source)
XLA Modules:
  0.0 122.3 jit_solution(10813655550373398990)
XLA Ops:
  0.0 3.4 %convolution_convert_fusion.4 = bf16[64,1536]{1,0:T(8,128)(2,1)S(1)} fusion(bf16[1536,1536]{1,0:T(8,128)(2,1)} %param.9, bf16[1,64,1536]{2,1,0:T(8,128)(2,1)} %param.8), kind=kOutput, calls=%fused_computation.5 | convolution fusion | flops 302088192 | bytes 5111808 | tf_op jit(solution)/shard_map/dot_general | solution.py:50
  3.5 0.0 copy-start.2
  3.5 12.9 %all-gather = bf16[256,1536]{1,0:T(8,128)(2,1)S(1)} all-gather(bf16[64,1536]{1,0:T(8,128)(2,1)S(1)} %convolution_convert_fusion.4), channel_id=2, replica_groups=mesh['sector'=64,'dof'=4] {'dof'}, dimensions={0}, use_global_device_ids=true | all-gather | bytes 983040 | tf_op jit(solution)/shard_map/all_gather | solution.py:53
  16.4 0.1 reduce_sum.12
  16.5 0.3 copy.51
  16.9 0.6 broadcast.55
  17.5 1.8 %reduce.3 = bf16[64,1536]{1,0:T(8,128)(2,1)S(1)} reduce(bf16[64,1,1536]{2,1,0:T(2,128)(2,1)S(1)} %bitcast.51, bf16[]{:T(256)} %broadcast.55), dimensions={1}, to_apply=%bitcast.48.reduce_sub_computation | reduce | bytes 393218
  19.3 0.7 reshape.76
  20.0 13.9 %all-to-all-start = ((bf16[64,2,768]{2,1,0:T(2,128)(2,1)}), bf16[64,2,768]{2,1,0:T(2,128)(2,1)S(1)}, u32[]{:S(2)}, u32[]{:S(2)}) async-start(bf16[64,2,768]{2,1,0:T(2,128)(2,1)} %reshape.76), calls=%async_computation | async-start | bytes 393216 | tf_op jit(solution)/shard_map/all_to_all | solution.py:57
  34.6 11.3 %all-to-all-done = bf16[64,2,768]{2,1,0:T(2,128)(2,1)S(1)} async-done(((bf16[64,2,768]{2,1,0:T(2,128)(2,1)}), bf16[64,2,768]{2,1,0:T(2,128)(2,1)S(1)}, u32[]{:S(2)}, u32[]{:S(2)}) %all-to-all-start) | async-done | bytes 196640 | tf_op jit(solution)/shard_map/all_to_all | solution.py:57
  45.9 0.1 reshape.77
  46.1 0.5 fusion
  46.6 0.8 reduce.4
  47.4 0.7 reshape.78
  48.1 4.5 %all-to-all-start.1 = ((bf16[64,2,768]{2,1,0:T(2,128)(2,1)}), bf16[64,2,768]{2,1,0:T(2,128)(2,1)S(1)}, u32[]{:S(2)}, u32[]{:S(2)}) async-start(bf16[64,2,768]{2,1,0:T(2,128)(2,1)} %reshape.78), calls=%async_computation.1 | async-start | bytes 393216 | tf_op jit(solution)/shard_map/all_to_all | solution.py:62
  52.6 12.2 %all-to-all-done.1 = bf16[64,2,768]{2,1,0:T(2,128)(2,1)S(1)} async-done(((bf16[64,2,768]{2,1,0:T(2,128)(2,1)}), bf16[64,2,768]{2,1,0:T(2,128)(2,1)S(1)}, u32[]{:S(2)}, u32[]{:S(2)}) %all-to-all-start.1) | async-done | bytes 196640 | tf_op jit(solution)/shard_map/all_to_all | solution.py:62
  64.8 0.1 reshape.79
  65.0 0.2 fusion.4
  65.2 16.2 %multiply_reduce_fusion = bf16[256,64]{0,1:T(8,128)(2,1)S(1)} fusion(f32[256,64]{0,1:T(8,128)S(1)} %fusion.4, f32[256]{0:T(256)S(1)} %bitcast.58, f32[64,64]{1,0:T(8,128)S(1)} %maximum_convert_fusion, f32[256]{0:T(256)S(1)} %bitcast.57, f32[256]{0:T(256)S(1)} %bitcast.56, pred[64,64]{1,0:T(8,128)(4,1)S(1)} %fusion.20), kind=kLoop, calls=%fused_computation | loop fusion | flops 7323648 | bytes 121856
  81.5 0.1 copy.26
  81.6 0.4 fusion.1
  81.9 0.3 copy.50
  82.3 1.8 %reduce.5 = bf16[64,1536]{1,0:T(8,128)(2,1)S(1)} reduce(bf16[64,1,1536]{2,1,0:T(2,128)(2,1)S(1)} %bitcast.52, bf16[]{:T(256)} %broadcast.55), dimensions={1}, to_apply=%bitcast.47.reduce_sub_computation | reduce | bytes 393218
  84.1 0.1 reshape.80
  84.2 16.2 %all_to_all.16 = bf16[64,2,768]{2,1,0:T(2,128)(2,1)S(1)} all-to-all(bf16[64,2,768]{2,1,0:T(2,128)(2,1)S(1)} %reshape.80), channel_id=1, replica_groups=mesh['sector'=64,'dof'=4] {'sector'}, dimensions={0} | all-to-all | bytes 393216 | tf_op jit(solution)/shard_map/all_to_all | solution.py:75
  100.3 0.1 reshape.81
  100.5 0.6 fusion.2
  101.1 0.8 reduce.6
  101.8 0.1 reshape.82
  101.9 16.3 %all_to_all.17 = bf16[64,2,768]{2,1,0:T(2,128)(2,1)S(1)} all-to-all(bf16[64,2,768]{2,1,0:T(2,128)(2,1)S(1)} %reshape.82), channel_id=1, replica_groups=mesh['sector'=64,'dof'=4] {'sector'}, dimensions={0} | all-to-all | bytes 393216 | tf_op jit(solution)/shard_map/all_to_all | solution.py:80
  118.2 0.1 reshape.83
  118.3 3.9 %fusion.3 = bf16[1,64,1536]{2,1,0:T(8,128)(2,1)} fusion(bf16[1536,1536]{1,0:T(8,128)(2,1)} %param.11, bf16[64,1,1536]{2,1,0:T(2,128)(2,1)S(1)} %reshape.83), kind=kOutput, calls=%fused_computation.9 | convolution fusion | flops 302088192 | bytes 5111808 | tf_op jit(solution)/shard_map/dot_general | solution.py:83
  (14 shorter events, 0.1 us)
Async XLA Ops:
  0.0 64.9 %copy-start = (bf16[1,1536,256]{2,1,0:T(8,128)(2,1)S(1)}, bf16[1,1536,256]{2,1,0:T(8,128)(2,1)}, u32[]{:S(2)}) copy-start(bf16[1,1536,256]{2,1,0:T(8,128)(2,1)} %param.10) | copy-start | bytes 2359300
  0.0 33.9 %copy-start.3 = (s32[64]{0:T(128)S(1)}, s32[64]{0:T(128)}, u32[]{:S(2)}) copy-start(s32[64]{0:T(128)} %param.15) | copy-start | bytes 772
  3.5 49.2 %copy-start.1 = (f32[1,256]{1,0:T(1,128)S(1)}, f32[1,256]{1,0:T(1,128)}, u32[]{:S(2)}) copy-start(f32[1,256]{1,0:T(1,128)} %param.12) | copy-start | bytes 3076
  3.5 61.7 %copy-start.2 = (f32[1,256]{1,0:T(1,128)S(1)}, f32[1,256]{1,0:T(1,128)}, u32[]{:S(2)}) copy-start(f32[1,256]{1,0:T(1,128)} %param.13) | copy-start | bytes 3076
  20.0 25.9 %all-to-all-start = ((bf16[64,2,768]{2,1,0:T(2,128)(2,1)}), bf16[64,2,768]{2,1,0:T(2,128)(2,1)S(1)}, u32[]{:S(2)}, u32[]{:S(2)}) async-start(bf16[64,2,768]{2,1,0:T(2,128)(2,1)} %reshape.76), calls=%async_computation | async-start | bytes 393216 | tf_op jit(solution)/shard_map/all_to_all | solution.py:57
  48.1 16.7 %all-to-all-start.1 = ((bf16[64,2,768]{2,1,0:T(2,128)(2,1)}), bf16[64,2,768]{2,1,0:T(2,128)(2,1)S(1)}, u32[]{:S(2)}, u32[]{:S(2)}) async-start(bf16[64,2,768]{2,1,0:T(2,128)(2,1)} %reshape.78), calls=%async_computation.1 | async-start | bytes 393216 | tf_op jit(solution)/shard_map/all_to_all | solution.py:62
